TPU v7x, 32 devices: a whole 2x2x4 slice. The times are simulated.
32 devices in a mesh: bin: 2 (over y), row: 4 (over x, core), col: 4 (over z).
Axes of the slice: x: 2, y: 2, z: 4, core: 2. Of those that a mesh axis runs over, the one named last changes fastest.
Arguments:
- snapshots: bfloat16 [4096, 16, 64], P('row', 'bin', 'col'), may hold values from -6 to 6
- focus_in: bfloat16 [16, 4096, 128], P('bin', 'row'), may hold values from -0.09375 to 0.09375
- focus_out: bfloat16 [16, 4096, 128], P('bin', 'row'), may hold values from -0.5 to 0.5
- start_basis: float32 [4096, 128], replicated, may hold values from -6 to 6
Outputs:
- covariance: float32 [4096, 4096], P('col', 'row')
- basis_out: float32 [4096, 128], P(('row', 'col'))
All inputs are finite; a program needn't handle non-finite values.
Results may differ from a plain program's by a relative error of at most 0.0045.
Values may be sent and summed in bfloat16 or wider, within the bound.
No kernel may reach another device: no remote copies, remote signals or barrier semaphores. Data moves between devices by JAX's collectives and lax.ppermute only.
A program may use at most 128 MiB of HBM per device.

v0:
```python
import math
import jax
import jax.numpy as jnp
from jax import lax
from jax.sharding import PartitionSpec as P

ITERS = 2


def _transpose_pairs(row_count, col_count):
    return [
        (i * col_count + j, j * row_count + i)
        for i in range(row_count)
        for j in range(col_count)
        if i != j
    ]


def _qr_step(image, gram_axis):
    gram_part = jnp.dot(
        image.T, image, precision=lax.Precision.HIGHEST, preferred_element_type=jnp.float32
    )
    gram_matrix = lax.psum(gram_part, gram_axis)
    lower_factor = jnp.linalg.cholesky(gram_matrix)
    return jax.scipy.linalg.solve_triangular(lower_factor, image.T, lower=True).T


def shards(snapshots, focus_in, focus_out, start_basis):
    rows_here, bins_here, snaps_here = snapshots.shape
    bin_count = lax.axis_size("bin")
    row_count = lax.axis_size("row")
    col_count = lax.axis_size("col")
    col_here = lax.axis_index("col")
    row_here = lax.axis_index("row")
    partial_proj = jnp.einsum(
        "mbs,bmr->brs", snapshots, focus_in, preferred_element_type=jnp.float32
    )
    projected = lax.psum(partial_proj, "row").astype(jnp.bfloat16)
    lifted = jnp.einsum("bmr,brs->mbs", focus_out, projected, preferred_element_type=jnp.float32)
    focused = (snapshots.astype(jnp.float32) + lifted).astype(jnp.bfloat16)
    columns = bins_here * snaps_here
    local_rows = focused.reshape(rows_here, columns)
    array_size = rows_here * row_count
    col_block = array_size // col_count
    scaling = 1.0 / (columns * col_count * bin_count)
    right_rows = lax.all_gather(local_rows, ("bin", "col"), axis=0, tiled=False)
    if row_count == col_count:
        swapped = lax.ppermute(local_rows, ("row", "col"), _transpose_pairs(row_count, col_count))
        swapped = jnp.where(row_here == col_here, local_rows, swapped)
        left_rows = lax.all_gather(swapped, ("bin", "row"), axis=0, tiled=False)
    else:
        every_row = lax.all_gather(right_rows, "row", axis=1, tiled=True)
        left_rows = lax.dynamic_slice_in_dim(every_row, col_here * col_block, col_block, 1)
    covariance = (
        lax.dot_general(
            left_rows, right_rows, (((0, 2), (0, 2)), ((), ())), preferred_element_type=jnp.float32
        )
        * scaling
    )
    basis_rows = lax.dynamic_slice_in_dim(start_basis, row_here * rows_here, rows_here, 0)
    on_rows = True
    for sweep_index in range(ITERS):
        if on_rows:
            partial_image = jnp.dot(
                covariance,
                basis_rows,
                precision=lax.Precision.HIGHEST,
                preferred_element_type=jnp.float32,
            )
            image = lax.psum(partial_image, "row")
            basis_rows = _qr_step(image, "col")
        else:
            partial_image = lax.dot_general(
                covariance,
                basis_rows,
                (((0,), (0,)), ((), ())),
                precision=lax.Precision.HIGHEST,
                preferred_element_type=jnp.float32,
            )
            image = lax.psum(partial_image, "col")
            basis_rows = _qr_step(image, "row")
        on_rows = not on_rows
    if not on_rows:
        swapped = lax.ppermute(basis_rows, ("row", "col"), _transpose_pairs(row_count, col_count))
        basis_rows = jnp.where(row_here == col_here, basis_rows, swapped)
    out_rows = array_size // (row_count * col_count)
    basis_out = lax.dynamic_slice_in_dim(basis_rows, col_here * out_rows, out_rows, 0) * math.sqrt(
        array_size
    )
    return (covariance, basis_out)


def solution(mesh):
    in_specs = (P("row", "bin", "col"), P("bin", "row", None), P("bin", "row", None), P())
    out_specs = (P("col", "row"), P(("row", "col"), None))
    return jax.shard_map(shards, mesh=mesh, in_specs=in_specs, out_specs=out_specs, check_vma=False)
```

profile of v0, /device:TPU:0, one launch (start us, length us, event | category | flops | bytes accessed | tf_op | source)
XLA Modules:
  0.0 343.7 jit_solution(17615606288194781556)
XLA Ops:
  7.2 2.2 fusion.21
  9.4 13.4 %psum.35 = bf16[8,128,16]{1,2,0:T(8,128)(2,1)S(1)} all-reduce(f32[8,128,16]{1,2,0:T(8,128)S(1)} %fusion.21), channel_id=1, replica_groups=mesh['bin'=2,'row'=4,'col'=4] {'row'}, use_global_device_ids=true, to_apply=%region_0.0 | all-reduce | flops 16384 | bytes 98304 | tf_op jit(solution)/shard_map/psum | solution.py:38
  22.9 0.6 fusion.1
  23.6 0.7 collective-permute-start
  24.3 0.8 broadcast_select_fusion
  25.1 0.8 copy.14
  26.0 42.0 %all-gather.6.cloned.1.call-done = bf16[8192,128]{0,1:T(8,128)(2,1)} async-done(((bf16[1024,128]{0,1:T(8,128)(2,1)}), bf16[8192,128]{0,1:T(8,128)(2,1)}) %all-gather.6.cloned.1.call-update) | async-done | bytes 2097168 | tf_op jit(solution)/shard_map/all_gather | solution.py:50
  68.0 4.1 %copy.13 = bf16[8192,128]{1,0:T(8,128)(2,1)} copy(bf16[8192,128]{0,1:T(8,128)(2,1)} %all-gather.6.cloned.1.call-done) | data formatting | bytes 4194304 | tf_op jit(solution)/shard_map/all_gather | solution.py:50
  72.0 47.2 %all-gather.4.cloned.1.call-done = bf16[8,1024,128]{2,1,0:T(8,128)(2,1)} async-done(((bf16[1,1024,128]{2,1,0:T(8,128)(2,1)}), bf16[8,1024,128]{2,1,0:T(8,128)(2,1)}) %all-gather.4.cloned.1.call-update) | async-done | bytes 2097168 | tf_op jit(solution)/shard_map/all_gather | solution.py:46
  119.2 4.6 %bitcast_multiply_fusion = f32[1024,1024]{1,0:T(8,128)S(1)} fusion(bf16[8,1024,128]{2,1,0:T(8,128)(2,1)} %bitcast.53, bf16[8,1024,128]{2,1,0:T(8,128)(2,1)} %all-gather.4.cloned.1.call-done), kind=kOutput, calls=%fused_computation | convolution fusion | flops 2148532224 | bytes 8388608 | tf_op jit(solution)/shard_map/dot_general | solution.py:55
  123.8 2.0 copy-done.1
  125.8 5.3 %fusion.6 = f32[1024,128]{1,0:T(8,128)} fusion(f32[1024,1024]{1,0:T(8,128)S(1)} %bitcast_multiply_fusion, f32[4096,128]{1,0:T(8,128)} %param.10, s32[]{:T(128)S(6)} %select_n.19), kind=kOutput, calls=%fused_computation.8 | convolution fusion | flops 1610612736 | bytes 5242884 | tf_op jit(solution)/shard_map/dot_general | solution.py:64
  131.2 32.0 %all-reduce.5.cloned.1.call-done = f32[1024,128]{1,0:T(8,128)} async-done(((f32[1024,128]{1,0:T(8,128)}), f32[1024,128]{1,0:T(8,128)}) %all-reduce.5.cloned.1.call-update) | async-done | bytes 524304 | tf_op jit(solution)/shard_map/psum | solution.py:70
  163.2 2.8 fusion.18
  166.3 34.3 %all-reduce.7.cloned.1.call-done = f32[128,128]{0,1:T(8,128)} async-done(((f32[128,128]{0,1:T(8,128)}), f32[128,128]{0,1:T(8,128)}) %all-reduce.7.cloned.1.call-update) | async-done | bytes 65552 | tf_op jit(solution)/shard_map/psum | solution.py:23
  200.6 0.9 copy.16
  201.5 0.9 fusion.13
  202.4 11.7 %cholesky.44 = f32[128,128]{1,0:T(8,128)S(1)} custom-call(f32[128,128]{1,0:T(8,128)S(1)} %fusion.13), custom_call_target="Cholesky" | custom-call | tf_op jit(solution)/shard_map/jit(cholesky)/cholesky | solution.py:24
  214.8 0.7 fusion.8
  215.5 9.8 %custom-call.6 = f32[1,128,128]{1,2,0:T(8,128)S(1)} custom-call(f32[1,128,128]{2,1,0:T(8,128)S(1)} %fusion.8), custom_call_target="InvertDiagBlocksLowerTriangular" | custom-call | tf_op jit(solution)/shard_map/jit(_solve_triangular)/triangular_solve | solution.py:25
  225.3 1.7 fusion.4
  227.0 9.9 %fusion.19 = f32[1024,128]{1,0:T(8,128)} fusion(f32[1024,1024]{1,0:T(8,128)} %copy-done.1, f32[128,1024]{1,0:T(8,128)S(1)} %fusion.4), kind=kOutput, calls=%fused_computation.32 | convolution fusion | flops 1610612736 | bytes 5242880 | tf_op jit(solution)/shard_map/dot_general | solution.py:73
  236.9 38.5 %all-reduce.9.cloned.1.call-done = f32[1024,128]{1,0:T(8,128)} async-done(((f32[1024,128]{1,0:T(8,128)}), f32[1024,128]{1,0:T(8,128)}) %all-reduce.9.cloned.1.call-update) | async-done | bytes 524304 | tf_op jit(solution)/shard_map/psum | solution.py:80
  275.4 2.8 fusion.20
  278.2 31.5 %all-reduce.11.cloned.1.call-done = f32[128,128]{0,1:T(8,128)} async-done(((f32[128,128]{0,1:T(8,128)}), f32[128,128]{0,1:T(8,128)}) %all-reduce.11.cloned.1.call-update) | async-done | bytes 65552 | tf_op jit(solution)/shard_map/psum | solution.py:23
  309.7 0.9 copy.18
  310.7 0.9 fusion.11
  311.5 11.7 %cholesky.55 = f32[128,128]{1,0:T(8,128)S(1)} custom-call(f32[128,128]{1,0:T(8,128)S(1)} %fusion.11), custom_call_target="Cholesky" | custom-call | tf_op jit(solution)/shard_map/jit(cholesky)/cholesky | solution.py:24
  323.9 0.7 fusion.9
  324.6 9.8 %custom-call.7 = f32[1,128,128]{1,2,0:T(8,128)S(1)} custom-call(f32[1,128,128]{2,1,0:T(8,128)S(1)} %fusion.9), custom_call_target="InvertDiagBlocksLowerTriangular" | custom-call | tf_op jit(solution)/shard_map/jit(_solve_triangular)/triangular_solve | solution.py:25
  334.4 1.7 fusion.2
  336.1 0.8 copy.19
  (23 shorter events, 1.9 us)
Async XLA Ops:
  7.2 15.7 %copy-start = (bf16[8,1024,128]{2,1,0:T(8,128)(2,1)S(1)}, bf16[8,1024,128]{2,1,0:T(8,128)(2,1)}, u32[]{:S(2)}) copy-start(bf16[8,1024,128]{2,1,0:T(8,128)(2,1)} %param.9) | copy-start | bytes 6291460
  7.2 15.7 %copy-start.2 = (bf16[1024,8,16]{0,2,1:T(8,128)(2,1)S(1)}, bf16[1024,8,16]{0,2,1:T(8,128)(2,1)}, u32[]{:S(2)}) copy-start(bf16[1024,8,16]{0,2,1:T(8,128)(2,1)} %param.7) | copy-start | bytes 786436
  7.2 60.8 %all-gather.6.cloned.1.call-start = ((), (), s32[]{:S(2)}) async-start(), calls=%async_computation.5 | async-start | bytes 2359296 | tf_op jit(solution)/shard_map/all_gather | solution.py:50
  23.6 0.7 collective-permute-start
  25.0 94.2 %all-gather.4.cloned.1.call-start = ((), (), s32[]{:S(2)}) async-start(), calls=%async_computation | async-start | bytes 2359296 | tf_op jit(solution)/shard_map/all_gather | solution.py:46
  25.9 137.3 %all-reduce.5.cloned.1.call-start = ((), (), s32[]{:S(2)}) async-start(), calls=%async_computation.1 | async-start | bytes 1048576 | tf_op jit(solution)/shard_map/psum | solution.py:70
  123.8 2.0 copy-start.1
  131.1 69.5 %all-reduce.7.cloned.1.call-start = ((), (), s32[]{:S(2)}) async-start(), calls=%async_computation.2 | async-start | bytes 131072 | tf_op jit(solution)/shard_map/psum | solution.py:23
  166.0 109.3 %all-reduce.9.cloned.1.call-start = ((), (), s32[]{:S(2)}) async-start(), calls=%async_computation.3 | async-start | bytes 1048576 | tf_op jit(solution)/shard_map/psum | solution.py:80
  236.9 72.9 %all-reduce.11.cloned.1.call-start = ((), (), s32[]{:S(2)}) async-start(), calls=%async_computation.4 | async-start | bytes 131072 | tf_op jit(solution)/shard_map/psum | solution.py:23
Sparse Core Ops, SparseCore 0:
  25.2 42.7 all-gather.5
  70.1 49.0 all-gather.3
  131.2 31.9 all-reduce.4
  166.2 34.3 all-reduce.6
  237.0 38.3 all-reduce.8
  278.4 31.3 all-reduce.10
where the time goes:
time: 344 us
  waiting for transfers between devices  226 us (66%)
  other arithmetic  48.2 us (14%)
  matrix products  31.6 us (9%)
  between operations  14.3 us (4%)
  blocking collectives  13.4 us (4%)
  local copies, waits for them, and re-layouts  9.52 us (3%)
    psum x2, waiting for transfers between devices, _qr_step(): gram_matrix = lax.psum(gram_part, gram_axis)  65.8 us
    all_gather x1, waiting for transfers between devices, shards(): right_rows = lax.all_gather(local_rows, ('bin', 'col'), axis=0, tiled=False)  47.2 us
    all_gather x1, waiting for transfers between devices, shards(): left_rows = lax.all_gather(swapped, ('bin', 'row'), axis=0, tiled=False)  42 us
    psum x1, waiting for transfers between devices, shards(): image = lax.psum(partial_image, 'col')  38.5 us
    psum x1, waiting for transfers between devices, shards(): image = lax.psum(partial_image, 'row')  32 us
    another operation x6, other arithmetic, _qr_step(): lower_factor = jnp.linalg.cholesky(gram_matrix)  24.8 us
    another operation x4, other arithmetic, _qr_step(): jax.scipy.linalg.solve_triangular(lower_factor, image.T, lower=True)  20.9 us
    psum x1, blocking collectives, shards(): projected = lax.psum(partial_proj, 'row').astype(jnp.bfloat16)  13.4 us
  transfers between devices with their start and end apart: 7, of which 6 were waited for; matrix products, arithmetic and copies ran while one was open for 1% of the time, Pallas kernels for 0%

commit v1 on v0

--- a/solution.py
+++ b/solution.py
@@ -67,7 +67,9 @@
                 precision=lax.Precision.HIGHEST,
                 preferred_element_type=jnp.float32,
             )
-            image = lax.psum(partial_image, "row")
+            image = partial_image
+            for hop in (1, 2):
+                image = image + lax.ppermute(image, "row", [(dev, dev ^ hop) for dev in range(4)])
             basis_rows = _qr_step(image, "col")
         else:
             partial_image = lax.dot_general(

time: 344 us -> 322 us (0.936)
  waiting for transfers between devices: 226 us -> 206 us
    psum x1 -> x0, waiting for transfers between devices: 32 us -> none  [shards(): image = lax.psum(partial_image, 'row')]
    ppermute x0 -> x2, waiting for transfers between devices: none -> 14.4 us  [shards(): lax.ppermute(image, 'row', [(dev, dev ^ hop) for dev in range(4)])]
  transfers between devices with their start and end apart: 7 -> 8, of which waited for: 6 -> 7; matrix products, arithmetic and copies ran while one was open for 1% -> 2% of each run, Pallas kernels for 0% -> 0%
where the time goes in v1:
time: 322 us; the launch traced here: 321 us
  waiting for transfers between devices  206 us (64%)
  other arithmetic  48.2 us (15%)
  matrix products  29 us (9%)
  between operations  14 us (4%)
  blocking collectives  13.4 us (4%)
  local copies, waits for them, and re-layouts  7.51 us (2%)
    psum x2, waiting for transfers between devices, _qr_step(): gram_matrix = lax.psum(gram_part, gram_axis)  64.3 us
    all_gather x1, waiting for transfers between devices, shards(): right_rows = lax.all_gather(local_rows, ('bin', 'col'), axis=0, tiled=False)  47.2 us
    all_gather x1, waiting for transfers between devices, shards(): left_rows = lax.all_gather(swapped, ('bin', 'row'), axis=0, tiled=False)  42 us
    psum x1, waiting for transfers between devices, shards(): image = lax.psum(partial_image, 'col')  38.4 us
    another operation x6, other arithmetic, _qr_step(): lower_factor = jnp.linalg.cholesky(gram_matrix)  24.8 us
    another operation x4, other arithmetic, _qr_step(): jax.scipy.linalg.solve_triangular(lower_factor, image.T, lower=True)  20.9 us
    ppermute x2, waiting for transfers between devices, shards(): lax.ppermute(image, 'row', [(dev, dev ^ hop) for dev in range(4)])  14.4 us
    psum x1, blocking collectives, shards(): projected = lax.psum(partial_proj, 'row').astype(jnp.bfloat16)  13.4 us
  transfers between devices with their start and end apart: 8, of which 7 were waited for; matrix products, arithmetic and copies ran while one was open for 2% of the time, Pallas kernels for 0%

profile of v1, /device:TPU:0, one launch (start us, length us, event | category | flops | bytes accessed | tf_op | source)
XLA Modules:
  0.0 321.2 jit_solution(5326700686500446899)
XLA Ops:
  7.2 2.2 fusion.23
  9.4 13.4 %psum.28 = bf16[8,128,16]{1,2,0:T(8,128)(2,1)S(1)} all-reduce(f32[8,128,16]{1,2,0:T(8,128)S(1)} %fusion.23), channel_id=1, replica_groups=mesh['bin'=2,'row'=4,'col'=4] {'row'}, use_global_device_ids=true, to_apply=%region_0.0 | all-reduce | flops 16384 | bytes 98304 | tf_op jit(solution)/shard_map/psum | solution.py:38
  22.9 0.6 fusion.1
  23.6 0.7 collective-permute-start
  24.3 0.8 broadcast_select_fusion
  25.1 0.8 copy.14
  26.0 42.0 %all-gather.6.cloned.1.call-done = bf16[8192,128]{0,1:T(8,128)(2,1)} async-done(((bf16[1024,128]{0,1:T(8,128)(2,1)}), bf16[8192,128]{0,1:T(8,128)(2,1)}) %all-gather.6.cloned.1.call-update) | async-done | bytes 2097168 | tf_op jit(solution)/shard_map/all_gather | solution.py:50
  68.0 4.1 %copy.13 = bf16[8192,128]{1,0:T(8,128)(2,1)} copy(bf16[8192,128]{0,1:T(8,128)(2,1)} %all-gather.6.cloned.1.call-done) | data formatting | bytes 4194304 | tf_op jit(solution)/shard_map/all_gather | solution.py:50
  72.0 47.2 %all-gather.4.cloned.1.call-done = bf16[8,1024,128]{2,1,0:T(8,128)(2,1)} async-done(((bf16[1,1024,128]{2,1,0:T(8,128)(2,1)}), bf16[8,1024,128]{2,1,0:T(8,128)(2,1)}) %all-gather.4.cloned.1.call-update) | async-done | bytes 2097168 | tf_op jit(solution)/shard_map/all_gather | solution.py:46
  119.2 4.6 %bitcast_multiply_fusion = f32[1024,1024]{1,0:T(8,128)S(1)} fusion(bf16[8,1024,128]{2,1,0:T(8,128)(2,1)} %bitcast.51, bf16[8,1024,128]{2,1,0:T(8,128)(2,1)} %all-gather.4.cloned.1.call-done), kind=kOutput, calls=%fused_computation | convolution fusion | flops 2148532224 | bytes 8388608 | tf_op jit(solution)/shard_map/dot_general | solution.py:55
  123.8 4.9 %fusion.6 = f32[1024,128]{1,0:T(8,128)S(1)} fusion(f32[1024,1024]{1,0:T(8,128)S(1)} %bitcast_multiply_fusion, f32[4096,128]{1,0:T(8,128)} %param.10, s32[]{:T(128)S(6)} %select_n.19), kind=kOutput, calls=%fused_computation.8 | convolution fusion | flops 1610612736 | bytes 5242884 | tf_op jit(solution)/shard_map/dot_general | solution.py:64
  128.8 1.9 collective-permute-done.1
  130.7 1.5 collective-permute-start.2
  132.3 12.5 %collective-permute-done.2 = f32[1024,128]{1,0:T(8,128)S(1)} collective-permute-done((f32[1024,128]{1,0:T(8,128)S(1)}, f32[1024,128]{1,0:T(8,128)S(1)}, u32[]{:S(2)}, u32[]{:S(2)}) %collective-permute-start.2) | collective-permute-done | bytes 524320 | tf_op jit(solution)/shard_map/ppermute | solution.py:72
  144.8 1.6 fusion.9
  146.7 32.8 %all-reduce.4.cloned.1.call-done = f32[128,128]{0,1:T(8,128)} async-done(((f32[128,128]{0,1:T(8,128)}), f32[128,128]{0,1:T(8,128)}) %all-reduce.4.cloned.1.call-update) | async-done | bytes 65552 | tf_op jit(solution)/shard_map/psum | solution.py:23
  179.4 0.9 copy.16
  180.4 0.9 fusion.16
  181.2 11.7 %cholesky.44 = f32[128,128]{1,0:T(8,128)S(1)} custom-call(f32[128,128]{1,0:T(8,128)S(1)} %fusion.16), custom_call_target="Cholesky" | custom-call | tf_op jit(solution)/shard_map/jit(cholesky)/cholesky | solution.py:24
  193.6 0.7 fusion.11
  194.3 9.8 %custom-call.6 = f32[1,128,128]{1,2,0:T(8,128)S(1)} custom-call(f32[1,128,128]{2,1,0:T(8,128)S(1)} %fusion.11), custom_call_target="InvertDiagBlocksLowerTriangular" | custom-call | tf_op jit(solution)/shard_map/jit(_solve_triangular)/triangular_solve | solution.py:25
  204.7 9.9 %fusion.21 = f32[1024,128]{1,0:T(8,128)} fusion(f32[1024,1024]{1,0:T(8,128)} %copy-done.1, f32[128,1024]{1,0:T(8,128)S(1)} %fusion.4), kind=kOutput, calls=%fused_computation.34 | convolution fusion | flops 1610612736 | bytes 5242880 | tf_op jit(solution)/shard_map/dot_general | solution.py:75
  214.7 38.4 %all-reduce.6.cloned.1.call-done = f32[1024,128]{1,0:T(8,128)} async-done(((f32[1024,128]{1,0:T(8,128)}), f32[1024,128]{1,0:T(8,128)}) %all-reduce.6.cloned.1.call-update) | async-done | bytes 524304 | tf_op jit(solution)/shard_map/psum | solution.py:82
  253.1 2.8 fusion.22
  256.0 31.5 %all-reduce.8.cloned.1.call-done = f32[128,128]{0,1:T(8,128)} async-done(((f32[128,128]{0,1:T(8,128)}), f32[128,128]{0,1:T(8,128)}) %all-reduce.8.cloned.1.call-update) | async-done | bytes 65552 | tf_op jit(solution)/shard_map/psum | solution.py:23
  287.5 0.9 copy.18
  288.4 0.9 fusion.14
  289.3 11.7 %cholesky.55 = f32[128,128]{1,0:T(8,128)S(1)} custom-call(f32[128,128]{1,0:T(8,128)S(1)} %fusion.14), custom_call_target="Cholesky" | custom-call | tf_op jit(solution)/shard_map/jit(cholesky)/cholesky | solution.py:24
  301.7 0.7 fusion.12
  302.3 9.8 %custom-call.7 = f32[1,128,128]{1,2,0:T(8,128)S(1)} custom-call(f32[1,128,128]{2,1,0:T(8,128)S(1)} %fusion.12), custom_call_target="InvertDiagBlocksLowerTriangular" | custom-call | tf_op jit(solution)/shard_map/jit(_solve_triangular)/triangular_solve | solution.py:25
  312.2 1.7 fusion.2
  313.9 0.8 copy.19
  (25 shorter events, 2.6 us)
Async XLA Ops:
  7.2 15.7 %copy-start = (bf16[8,1024,128]{2,1,0:T(8,128)(2,1)S(1)}, bf16[8,1024,128]{2,1,0:T(8,128)(2,1)}, u32[]{:S(2)}) copy-start(bf16[8,1024,128]{2,1,0:T(8,128)(2,1)} %param.9) | copy-start | bytes 6291460
  7.2 15.7 %copy-start.2 = (bf16[1024,8,16]{0,2,1:T(8,128)(2,1)S(1)}, bf16[1024,8,16]{0,2,1:T(8,128)(2,1)}, u32[]{:S(2)}) copy-start(bf16[1024,8,16]{0,2,1:T(8,128)(2,1)} %param.7) | copy-start | bytes 786436
  7.2 60.8 %all-gather.6.cloned.1.call-start = ((), (), s32[]{:S(2)}) async-start(), calls=%async_computation.4 | async-start | bytes 2359296 | tf_op jit(solution)/shard_map/all_gather | solution.py:50
  23.6 0.7 collective-permute-start
  25.0 94.2 %all-gather.4.cloned.1.call-start = ((), (), s32[]{:S(2)}) async-start(), calls=%async_computation | async-start | bytes 2359296 | tf_op jit(solution)/shard_map/all_gather | solution.py:46
  25.9 153.5 %all-reduce.4.cloned.1.call-start = ((), (), s32[]{:S(2)}) async-start(), calls=%async_computation.1 | async-start | bytes 131072 | tf_op jit(solution)/shard_map/psum | solution.py:23
  123.8 4.9 %copy-start.1 = (f32[1024,1024]{1,0:T(8,128)}, f32[1024,1024]{1,0:T(8,128)S(1)}, u32[]{:S(2)}) copy-start(f32[1024,1024]{1,0:T(8,128)S(1)} %bitcast_multiply_fusion) | copy-start | bytes 12582916
  128.7 2.0 collective-permute-start.1
  130.7 14.0 %collective-permute-start.2 = (f32[1024,128]{1,0:T(8,128)S(1)}, f32[1024,128]{1,0:T(8,128)S(1)}, u32[]{:S(2)}, u32[]{:S(2)}) collective-permute-start(f32[1024,128]{1,0:T(8,128)S(1)} %add.34), channel_id=1, source_target_pairs={{0,8},{4,12},{8,0},{12,4},{1,9},{5,13},{9,1},{13,5},{2,10},{6,14},... | collective-permute-start | bytes 1572872 | tf_op jit(solution)/shard_map/ppermute | solution.py:72
  146.4 106.7 %all-reduce.6.cloned.1.call-start = ((), (), s32[]{:S(2)}) async-start(), calls=%async_computation.2 | async-start | bytes 1048576 | tf_op jit(solution)/shard_map/psum | solution.py:82
  214.6 72.9 %all-reduce.8.cloned.1.call-start = ((), (), s32[]{:S(2)}) async-start(), calls=%async_computation.3 | async-start | bytes 131072 | tf_op jit(solution)/shard_map/psum | solution.py:23
Sparse Core Ops, SparseCore 0:
  25.2 42.7 all-gather.5
  70.1 49.0 all-gather.3
  146.6 32.8 all-reduce.3
  214.8 38.3 all-reduce.5
  256.1 31.3 all-reduce.7
